TPU v7x, 32 devices: a whole 2x2x4 slice. The times are simulated.
32 devices in a mesh: pipe: 2 (over core), ep: 16 (over z, y, x).
Axes of the slice: x: 2, y: 2, z: 4, core: 2. Of those that a mesh axis runs over, the one named last changes fastest.
Arguments:
- x_fwd: bfloat16 [2, 1024, 2048], P('pipe', 'ep'), may hold values from -6 to 6
- ids_fwd: int32 [2, 1024, 8], P('pipe', 'ep'), may hold values from 0 to 15, all different within a row; in each aligned block of 64 rows (0 to 63, 64 to 127, ..., all dimensions but the last counted through in order) at most 48 rows name the same one
- route_fwd: float32 [2, 1024, 8], P('pipe', 'ep'), may hold values from 0.05 to 1
- x_bwd: bfloat16 [2, 1024, 2048], P('pipe', 'ep'), may hold values from -6 to 6
- grad_bwd: bfloat16 [2, 1024, 2048], P('pipe', 'ep'), may hold values from -6 to 6
- ids_bwd: int32 [2, 1024, 8], P('pipe', 'ep'), may hold values from 0 to 15, all different within a row; in each aligned block of 64 rows (0 to 63, 64 to 127, ..., all dimensions but the last counted through in order) at most 48 rows name the same one
- route_bwd: float32 [2, 1024, 8], P('pipe', 'ep'), may hold values from 0.05 to 1
- norm_gain: bfloat16 [2, 2048], P('pipe'), may hold values from 0.25 to 1.75
- w_gate: bfloat16 [2, 16, 2048, 768], P('pipe', 'ep'), may hold values from -0.125 to 0.125
- w_up: bfloat16 [2, 16, 2048, 768], P('pipe', 'ep'), may hold values from -0.125 to 0.125
- w_down: bfloat16 [2, 16, 768, 2048], P('pipe', 'ep'), may hold values from -0.21875 to 0.21875
Outputs:
- fwd_next: bfloat16 [2, 1024, 2048], P('pipe', 'ep')
- bwd_prev: bfloat16 [2, 1024, 2048], P('pipe', 'ep')
Inputs may be any that keep to these rules, and one draw needn't show every extreme that they name: `ids_fwd`: in each aligned block of 64 tokens of a section, each token names 8 different experts, no expert is named by more than 48 tokens, and in some block one expert is named by exactly 48. `ids_bwd`: as for ids_fwd.
All inputs are finite; a program needn't handle non-finite values.
Results may differ from a plain program's by a relative error of at most 0.0046.
Values may be sent and summed in bfloat16 or wider, within the bound.
No kernel may reach another device: no remote copies, remote signals or barrier semaphores. Data moves between devices by JAX's collectives and lax.ppermute only.
A program may use at most 128 MiB of HBM per device.

v0:
```python
import jax
import jax.numpy as jnp
from jax import lax
from jax.sharding import PartitionSpec as P

EPS = 1e-06


def from_behind(block, axis, distance):
    devices = range(lax.axis_size(axis))
    route = [((i - distance) % len(devices), i) for i in devices]
    return lax.ppermute(block, axis, route)


def slot_places(ids, n_exp, cap):
    flat = ids.reshape(-1)
    onehot = (flat[:, None] == jnp.arange(n_exp, dtype=jnp.int32)[None, :]).astype(jnp.int32)
    before = jnp.cumsum(onehot, axis=0) - onehot
    slot = jnp.sum(before * onehot, axis=1)
    return flat * cap + slot


def rms_stats(x):
    xf = x.astype(jnp.float32)
    scale = lax.rsqrt(jnp.mean(xf * xf, axis=-1, keepdims=True) + EPS)
    return (xf, scale)


def expert_forward(rows, w_g, w_u, w_d):
    gate = jnp.dot(rows, w_g, preferred_element_type=jnp.float32)
    upper = jnp.dot(rows, w_u, preferred_element_type=jnp.float32)
    act = (jax.nn.silu(gate) * upper).astype(jnp.bfloat16)
    return jnp.dot(act, w_d, preferred_element_type=jnp.float32).astype(jnp.bfloat16)


def expert_backward(rows, cot, w_g, w_u, w_d):
    gate = jnp.dot(rows, w_g, preferred_element_type=jnp.float32)
    upper = jnp.dot(rows, w_u, preferred_element_type=jnp.float32)
    sigma = jax.nn.sigmoid(gate)
    dact = jnp.dot(cot, w_d.T, preferred_element_type=jnp.float32)
    dgate = (dact * upper * sigma * (1.0 + gate * (1.0 - sigma))).astype(jnp.bfloat16)
    dup = (dact * gate * sigma).astype(jnp.bfloat16)
    total = jnp.dot(dgate, w_g.T, preferred_element_type=jnp.float32) + jnp.dot(
        dup, w_u.T, preferred_element_type=jnp.float32
    )
    return total.astype(jnp.bfloat16)


def norm_backward(xf, scale, gain, upstream):
    scaled = gain * upstream
    inner = jnp.mean(xf * scaled, axis=-1, keepdims=True)
    return scale * scaled - xf * (scale * scale * scale) * inner


def expert_slots(ids_all, weights_all, me, cap):
    match = ids_all == me
    chosen = jnp.any(match, axis=-1)
    weight = jnp.sum(jnp.where(match, weights_all, 0.0), axis=-1)
    pos = jnp.cumsum(chosen.astype(jnp.int32), axis=1) - chosen.astype(jnp.int32)
    slot = jnp.arange(cap, dtype=jnp.int32)[None, :, None]
    onehot = chosen[:, None, :] & (pos[:, None, :] == slot)
    slot_w = jnp.sum(jnp.where(onehot, weight[:, None, :], 0.0), axis=-1)
    return (onehot.astype(jnp.bfloat16), slot_w)


def pick_rows(onehot, rows):
    picked = jnp.einsum("bct,btd->bcd", onehot, rows, preferred_element_type=jnp.float32)
    return picked.astype(jnp.bfloat16)


def combine_rows(places, back, top):
    count = back.shape[0]
    onehot = (places[:, None] == jnp.arange(count, dtype=jnp.int32)[None, :]).astype(jnp.bfloat16)
    picked = jnp.dot(onehot, back, preferred_element_type=jnp.float32)
    return picked.reshape(-1, top, back.shape[1])


def _pairs(n, n2, stage, move):
    out = []
    for i in range(n):
        e1, e2 = (i // n2, i % n2)
        if stage == 1:
            e1 = move(e1)
        else:
            e2 = move(e2)
        out.append((i, e1 * n2 + e2))
    return out


def gather_ep(v, axis_name):
    n = lax.axis_size(axis_name)
    n2 = 4
    if n % n2 or v.shape[0] % 2:
        return lax.all_gather(v, axis_name, axis=0, tiled=False)
    n1 = n // n2
    me = lax.axis_index(axis_name)
    e1, e2 = (me // n2, me % n2)
    s1 = jnp.zeros((n1,) + v.shape, v.dtype)
    s1 = lax.dynamic_update_index_in_dim(s1, v, e1, 0)
    for d in range(1, n1):
        got = lax.ppermute(v, axis_name, _pairs(n, n2, 1, lambda a: (a + d) % n1))
        s1 = lax.dynamic_update_index_in_dim(s1, got, (e1 - d) % n1, 0)
    flip_x = lambda a: a ^ 1
    flip_y = lambda a: a ^ 2
    px = lax.ppermute(s1, axis_name, _pairs(n, n2, 2, flip_x))
    py = lax.ppermute(s1, axis_name, _pairs(n, n2, 2, flip_y))
    h = v.shape[0] // 2
    d1 = lax.ppermute(px[:, :h], axis_name, _pairs(n, n2, 2, flip_y))
    d2 = lax.ppermute(py[:, h:], axis_name, _pairs(n, n2, 2, flip_x))
    diag = jnp.concatenate([d1, d2], axis=1)
    s2 = jnp.zeros((n2,) + s1.shape, v.dtype)
    s2 = lax.dynamic_update_index_in_dim(s2, s1, e2, 0)
    s2 = lax.dynamic_update_index_in_dim(s2, px, e2 ^ 1, 0)
    s2 = lax.dynamic_update_index_in_dim(s2, py, e2 ^ 2, 0)
    s2 = lax.dynamic_update_index_in_dim(s2, diag, e2 ^ 3, 0)
    return jnp.swapaxes(s2, 0, 1).reshape((n,) + v.shape)


def local(
    x_fwd, ids_fwd, route_fwd, x_bwd, grad_bwd, ids_bwd, route_bwd, norm_gain, w_gate, w_up, w_down
):
    n_exp = lax.axis_size("ep")
    me = lax.axis_index("ep")
    tok_dev = x_fwd.shape[1]
    width = x_fwd.shape[2]
    top = ids_fwd.shape[2]
    cap = 3 * tok_dev * top // (2 * n_exp)
    gain = norm_gain[0].astype(jnp.float32)
    w_g = w_gate[0, 0]
    w_u = w_up[0, 0]
    w_d = w_down[0, 0]
    xf, scale_f = rms_stats(x_fwd[0])
    h_f = (xf * scale_f * gain).astype(jnp.bfloat16)
    xb, scale_b = rms_stats(x_bwd[0])
    h_b = (xb * scale_b * gain).astype(jnp.bfloat16)
    grad = grad_bwd[0]
    weights_f = route_fwd[0] / jnp.sum(route_fwd[0], axis=-1, keepdims=True)
    weights_b = route_bwd[0] / jnp.sum(route_bwd[0], axis=-1, keepdims=True)

    def split3(r):
        hi = lax.reduce_precision(r, exponent_bits=8, mantissa_bits=7)
        rest = r - hi
        mid = lax.reduce_precision(rest, exponent_bits=8, mantissa_bits=7)
        return jnp.concatenate([hi, mid, rest - mid], axis=-1).astype(jnp.bfloat16)

    def join3(p):
        p = p.astype(jnp.float32)
        return p[..., 0:top] + p[..., top : 2 * top] + p[..., 2 * top : 3 * top]

    meta = jnp.concatenate(
        [
            ids_fwd[0].astype(jnp.bfloat16),
            ids_bwd[0].astype(jnp.bfloat16),
            split3(route_fwd[0]),
            split3(route_bwd[0]),
        ],
        axis=-1,
    )
    pad = -meta.shape[-1] % 128
    meta = jnp.concatenate([meta, jnp.zeros((tok_dev, pad), jnp.bfloat16)], axis=-1)
    message = gather_ep(jnp.concatenate([h_f, h_b, grad, meta], axis=-1), "ep")
    all_h_f = message[..., 0:width]
    all_h_b = message[..., width : 2 * width]
    all_g = message[..., 2 * width : 3 * width]
    got = message[..., 3 * width :]
    all_ids_f = got[..., 0:top].astype(jnp.int32)
    all_ids_b = got[..., top : 2 * top].astype(jnp.int32)
    all_route_f = join3(got[..., 2 * top : 5 * top])
    all_route_b = join3(got[..., 5 * top : 8 * top])
    all_w_f = all_route_f / jnp.sum(all_route_f, axis=-1, keepdims=True)
    all_w_b = all_route_b / jnp.sum(all_route_b, axis=-1, keepdims=True)
    onehot_f, _ = expert_slots(all_ids_f, all_w_f, me, cap)
    rows = pick_rows(onehot_f, all_h_f).reshape(-1, width)
    made_f = expert_forward(rows, w_g, w_u, w_d).reshape(n_exp, cap, width)
    back_f = lax.all_to_all(made_f, "ep", split_axis=0, concat_axis=0, tiled=True)
    onehot_b, slot_w_b = expert_slots(all_ids_b, all_w_b, me, cap)
    rows = pick_rows(onehot_b, all_h_b).reshape(-1, width)
    g_rows = pick_rows(onehot_b, all_g)
    cots = (
        (slot_w_b[:, :, None] * g_rows.astype(jnp.float32)).astype(jnp.bfloat16).reshape(-1, width)
    )
    made_b = expert_backward(rows, cots, w_g, w_u, w_d).reshape(n_exp, cap, width)
    back_b = lax.all_to_all(made_b, "ep", split_axis=0, concat_axis=0, tiled=True)
    places_f = slot_places(ids_fwd[0], n_exp, cap)
    picked_f = combine_rows(places_f, back_f.reshape(-1, width), top)
    mixed = jnp.sum(weights_f[:, :, None] * picked_f, axis=1)
    layer_out = (xf + mixed).astype(jnp.bfloat16)[None]
    places_b = slot_places(ids_bwd[0], n_exp, cap)
    picked_b = combine_rows(places_b, back_b.reshape(-1, width), top)
    dnorm = jnp.sum(picked_b, axis=1)
    input_grad = (grad.astype(jnp.float32) + norm_backward(xb, scale_b, gain, dnorm)).astype(
        jnp.bfloat16
    )[None]
    fwd_next = from_behind(layer_out, "pipe", 1)
    bwd_prev = from_behind(input_grad, "pipe", -1)
    return (fwd_next, bwd_prev)


def solution(mesh):
    placed = (
        P("pipe", "ep", None),
        P("pipe", "ep", None),
        P("pipe", "ep", None),
        P("pipe", "ep", None),
        P("pipe", "ep", None),
        P("pipe", "ep", None),
        P("pipe", "ep", None),
        P("pipe", None),
        P("pipe", "ep", None, None),
        P("pipe", "ep", None, None),
        P("pipe", "ep", None, None),
    )
    return jax.shard_map(
        local,
        mesh=mesh,
        in_specs=placed,
        out_specs=(P("pipe", "ep", None), P("pipe", "ep", None)),
        check_vma=False,
    )
```

profile of v0, /device:TPU:13, one launch (start us, length us, event | category | flops | bytes accessed | tf_op | source)
XLA Modules:
  0.0 404.9 jit_solution(13965254821809151938)
XLA Ops:
  0.6 1.3 fusion.55
  1.9 1.1 fusion.59
  10.3 1.9 fusion.61
  12.8 2.0 concatenate.11
  14.8 1.3 collective-permute-start
  17.2 1.4 collective-permute-start.2
  18.6 1.9 broadcast_in_dim.77
  21.5 12.4 %collective-permute-done = bf16[64,6272]{1,0:T(8,128)(2,1)} collective-permute-done((bf16[64,6272]{1,0:T(8,128)(2,1)}, bf16[64,6272]{1,0:T(8,128)(2,1)}, u32[]{:S(2)}, u32[]{:S(2)}) %collective-permute-start) | collective-permute-done | bytes 802848 | tf_op jit(solution)/shard_map/ppermute | solution.py:101
  33.9 2.1 bitcast_dynamic-update-slice_fusion.5
  36.0 48.6 %collective-permute-done.1 = bf16[64,6272]{1,0:T(8,128)(2,1)} collective-permute-done((bf16[64,6272]{1,0:T(8,128)(2,1)}, bf16[64,6272]{1,0:T(8,128)(2,1)}, u32[]{:S(2)}, u32[]{:S(2)}) %collective-permute-start.1) | collective-permute-done | bytes 802848 | tf_op jit(solution)/shard_map/ppermute | solution.py:101
  84.6 2.1 bitcast_dynamic-update-slice_fusion.4
  87.5 2.1 bitcast_dynamic-update-slice_fusion.3
  89.5 1.2 collective-permute-start.3
  91.0 6.2 %broadcast_in_dim.76 = bf16[4,4,64,6272]{3,2,0,1:T(8,128)(2,1)} broadcast(bf16[]{:T(256)} %constant.89.clone.1), dimensions={} | broadcast | bytes 12845058 | tf_op jit(solution)/shard_map/broadcast_in_dim | solution.py:111
  97.2 3.8 bitcast_dynamic-update-slice_fusion.2
  101.0 59.1 %collective-permute-done.3 = bf16[4,64,6272]{2,1,0:T(8,128)(2,1)} collective-permute-done((bf16[4,64,6272]{2,1,0:T(8,128)(2,1)}, bf16[4,64,6272]{2,1,0:T(8,128)(2,1)}, u32[]{:S(2)}, u32[]{:S(2)}) %collective-permute-start.3) | collective-permute-done | bytes 3211296 | tf_op jit(solution)/shard_map/ppermute | solution.py:105
  160.1 1.5 slice.65
  161.9 1.5 slice.66
  163.5 1.3 collective-permute-start.6
  164.7 3.8 bitcast_dynamic-update-slice_fusion.1
  168.6 3.8 bitcast_dynamic-update-slice_fusion
  172.4 24.3 %collective-permute-done.5 = bf16[4,32,6272]{2,1,0:T(8,128)(2,1)S(1)} collective-permute-done((bf16[4,32,6272]{2,1,0:T(8,128)(2,1)S(1)}, bf16[4,32,6272]{2,1,0:T(8,128)(2,1)S(1)}, u32[]{:S(2)}, u32[]{:S(2)}) %collective-permute-start.5) | collective-permute-done | bytes 1605664 | tf_op jit(solution)/shard_map/ppermute | solution.py:108
  196.7 1.5 collective-permute-done.6
  198.2 1.9 fusion.16
  200.2 1.1 slice_convert_fusion
  201.3 1.9 fusion.88
  203.2 6.4 %fusion.95 = f32[16,64]{1,0:T(8,128)S(1)} fusion(f32[16,64,24]{2,1,0:T(8,128)S(1)} %slice_convert_fusion, s32[]{:T(128)S(6)} %axis_index.16, bf16[16,64,6272]{2,1,0:T(8,128)(2,1)} %bitcast.179), kind=kOutput, calls=%fused_computation.135 | output fusion | flops 57351 | bytes 1593348 | tf_op jit(solution)/shard_map/div | solution.py:171
  209.8 3.1 fusion.13
  213.2 4.1 %multiply_convert_fusion = bf16[16,48,2048]{2,1,0:T(8,128)(2,1)S(1)} fusion(f32[16,48]{1,0:T(8,128)S(1)} %select_reduce_fusion, bf16[16,64,6272]{2,1,0:T(8,128)(2,1)} %bitcast.181, s32[16,64]{1,0:T(8,128)S(1)} %convert_subtract_fusion, pred[16,64]{1,0:T(8,128)(4,1)S(1)} %get-tuple-element.2), kind=kOutput, calls=%fused_computation.2 | convolution fusion | flops 207716352 | bytes 7348224 | tf_op jit(solution)/shard_map/bct,btd->bcd/dot_general | solution.py:67
  217.3 4.1 %fusion.17 = f32[768,768]{1,0:T(8,128)} fusion(bf16[768,2048]{1,0:T(8,128)(2,1)S(1)} %bitcast.189, bf16[1,1,768,2048]{3,2,1,0:T(8,128)(2,1)S(1)} %copy-done.8), kind=kOutput, calls=%fused_computation.19 | convolution fusion | flops 2415919104 | bytes 8650752 | tf_op jit(solution)/shard_map/dot_general | solution.py:40
  221.4 4.0 fusion.27
  225.5 12.9 %fusion.25 = f32[768,2048]{1,0:T(8,128)} fusion(bf16[1,1,2048,768]{3,2,1,0:T(8,128)(2,1)} %param.19, f32[768,768]{1,0:T(8,128)} %fusion.27, f32[768,768]{1,0:T(8,128)} %fusion.17, bf16[768,2048]{1,0:T(8,128)(2,1)} %bitcast.184, bf16[1,1,2048,768]{3,2,1,0:T(8,128)(2,1)S(1)} %copy-done), kind=kOutput, calls=%fused_computation.27 | convolution fusion | flops 4837736448 | bytes 20447232 | tf_op jit(solution)/shard_map/dot_general | solution.py:43
  238.3 7.4 %add_convert_fusion = bf16[768,2048]{1,0:T(8,128)(2,1)} fusion(f32[768,2048]{1,0:T(8,128)} %fusion.25, bf16[1,1,2048,768]{3,2,1,0:T(8,128)(2,1)S(1)} %copy-done, f32[768,768]{1,0:T(8,128)} %fusion.17, f32[768,768]{1,0:T(8,128)} %fusion.27), kind=kOutput, calls=%fused_computation.1 | convolution fusion | flops 2422603776 | bytes 17301504 | tf_op jit(solution)/shard_map/dot_general | solution.py:43
  245.8 5.3 %all-to-all-start.1 = ((bf16[16,48,2048]{2,1,0:T(8,128)(2,1)}), bf16[16,48,2048]{2,1,0:T(8,128)(2,1)}, u32[]{:S(2)}, u32[]{:S(2)}) async-start(bf16[16,48,2048]{2,1,0:T(8,128)(2,1)} %bitcast.188), calls=%async_computation.1 | async-start | bytes 6291456 | tf_op jit(solution)/shard_map/all_to_all | solution.py:183
  251.3 3.1 fusion.7
  254.5 1.7 copy-done.4
  256.1 4.0 fusion.23
  260.2 11.9 %convolution_convert_fusion = bf16[768,2048]{1,0:T(8,128)(2,1)} fusion(bf16[1,1,768,2048]{3,2,1,0:T(8,128)(2,1)} %param.21, f32[768,768]{1,0:T(8,128)} %fusion.23, bf16[768,2048]{1,0:T(8,128)(2,1)} %bitcast.186, bf16[1,1,2048,768]{3,2,1,0:T(8,128)(2,1)} %param.19), kind=kOutput, calls=%fused_computation.13 | convolution fusion | flops 4836950016 | bytes 14942208 | tf_op jit(solution)/shard_map/dot_general | solution.py:33
  272.0 49.7 %all-to-all-done.1 = bf16[16,48,2048]{2,1,0:T(8,128)(2,1)} async-done(((bf16[16,48,2048]{2,1,0:T(8,128)(2,1)}), bf16[16,48,2048]{2,1,0:T(8,128)(2,1)}, u32[]{:S(2)}, u32[]{:S(2)}) %all-to-all-start.1) | async-done | bytes 3145760 | tf_op jit(solution)/shard_map/all_to_all | solution.py:183
  321.8 4.6 %all-to-all-start = ((bf16[16,48,2048]{2,1,0:T(8,128)(2,1)}), bf16[16,48,2048]{2,1,0:T(8,128)(2,1)}, u32[]{:S(2)}, u32[]{:S(2)}) async-start(bf16[16,48,2048]{2,1,0:T(8,128)(2,1)} %bitcast.187), calls=%async_computation | async-start | bytes 6291456 | tf_op jit(solution)/shard_map/all_to_all | solution.py:175
  326.8 1.2 reduce-window.16
  328.4 1.2 reduce-window.14
  330.1 4.4 %convolution_reduce_fusion = f32[64,2048]{1,0:T(8,128)S(1)} fusion(bf16[768,2048,1]{1,0,2:T(8,128)(2,1)} %bitcast.40, s32[64,8]{1,0:T(8,128)S(1)} %bitcast_add_fusion), kind=kOutput, calls=%fused_computation.37 | convolution fusion | flops 1611923456 | bytes 3672064 | tf_op jit(solution)/shard_map/dot_general | solution.py:74
  335.7 1.9 collective-permute-start.8
  337.5 58.8 %all-to-all-done = bf16[16,48,2048]{2,1,0:T(8,128)(2,1)} async-done(((bf16[16,48,2048]{2,1,0:T(8,128)(2,1)}), bf16[16,48,2048]{2,1,0:T(8,128)(2,1)}, u32[]{:S(2)}, u32[]{:S(2)}) %all-to-all-start) | async-done | bytes 3145760 | tf_op jit(solution)/shard_map/all_to_all | solution.py:175
  396.3 4.5 %multiply_reduce_fusion = f32[64,2048]{1,0:T(8,128)S(1)} fusion(bf16[768,2048,1]{1,0,2:T(8,128)(2,1)} %bitcast.31, f32[64,8]{1,0:T(8,128)S(1)} %copy.37, s32[64,8]{1,0:T(8,128)S(1)} %bitcast_add_fusion.1), kind=kOutput, calls=%fused_computation.9 | convolution fusion | flops 1612972032 | bytes 3674112 | tf_op jit(solution)/shard_map/dot_general | solution.py:74
  400.9 1.5 collective-permute-start.7
  402.3 1.2 collective-permute-done.7
  (73 shorter events, 15.8 us)
Async XLA Ops:
  0.6 224.8 %copy-start = (bf16[1,1,2048,768]{3,2,1,0:T(8,128)(2,1)S(1)}, bf16[1,1,2048,768]{3,2,1,0:T(8,128)(2,1)}, u32[]{:S(2)}) copy-start(bf16[1,1,2048,768]{3,2,1,0:T(8,128)(2,1)} %param.20) | copy-start | bytes 9437188
  14.8 19.1 %collective-permute-start = (bf16[64,6272]{1,0:T(8,128)(2,1)}, bf16[64,6272]{1,0:T(8,128)(2,1)}, u32[]{:S(2)}, u32[]{:S(2)}) collective-permute-start(bf16[64,6272]{1,0:T(8,128)(2,1)} %concatenate.11), channel_id=1, source_target_pairs={{0,4},{1,5},{2,6},{3,7},{4,8},{5,9},{6,10},{7,11},{8,12},{9,13},{1... | collective-permute-start | bytes 2408456 | tf_op jit(solution)/shard_map/ppermute | solution.py:101
  16.1 68.5 %collective-permute-start.1 = (bf16[64,6272]{1,0:T(8,128)(2,1)}, bf16[64,6272]{1,0:T(8,128)(2,1)}, u32[]{:S(2)}, u32[]{:S(2)}) collective-permute-start(bf16[64,6272]{1,0:T(8,128)(2,1)} %concatenate.11), channel_id=1, source_target_pairs={{0,8},{1,9},{2,10},{3,11},{4,12},{5,13},{6,14},{7,15},{8,0},{9,1},... | collective-permute-start | bytes 2408456 | tf_op jit(solution)/shard_map/ppermute | solution.py:101
  17.2 70.3 %collective-permute-start.2 = (bf16[64,6272]{1,0:T(8,128)(2,1)}, bf16[64,6272]{1,0:T(8,128)(2,1)}, u32[]{:S(2)}, u32[]{:S(2)}) collective-permute-start(bf16[64,6272]{1,0:T(8,128)(2,1)} %concatenate.11), channel_id=1, source_target_pairs={{0,12},{1,13},{2,14},{3,15},{4,0},{5,1},{6,2},{7,3},{8,4},{9,5},{1... | collective-permute-start | bytes 2408456 | tf_op jit(solution)/shard_map/ppermute | solution.py:101
  18.6 2.0 copy-start.2
  89.5 70.6 %collective-permute-start.3 = (bf16[4,64,6272]{2,1,0:T(8,128)(2,1)}, bf16[4,64,6272]{2,1,0:T(8,128)(2,1)}, u32[]{:S(2)}, u32[]{:S(2)}) collective-permute-start(bf16[4,64,6272]{2,1,0:T(8,128)(2,1)} %bitcast_dynamic-update-slice_fusion.3), channel_id=1, source_target_pairs={{0,1},{1,0},{2,3},{3,2},{4,5},{5,4},{6,7},{7,6},{8,9},{9,8},{10,11... | collective-permute-start | bytes 9633800 | tf_op jit(solution)/shard_map/ppermute | solution.py:105
  90.7 71.2 %collective-permute-start.4 = (bf16[4,64,6272]{2,1,0:T(8,128)(2,1)}, bf16[4,64,6272]{2,1,0:T(8,128)(2,1)}, u32[]{:S(2)}, u32[]{:S(2)}) collective-permute-start(bf16[4,64,6272]{2,1,0:T(8,128)(2,1)} %bitcast_dynamic-update-slice_fusion.3), channel_id=1, source_target_pairs={{0,2},{1,3},{2,0},{3,1},{4,6},{5,7},{6,4},{7,5},{8,10},{9,11},{10,... | collective-permute-start | bytes 9633800 | tf_op jit(solution)/shard_map/ppermute | solution.py:106
  161.6 35.0 %collective-permute-start.5 = (bf16[4,32,6272]{2,1,0:T(8,128)(2,1)S(1)}, bf16[4,32,6272]{2,1,0:T(8,128)(2,1)S(1)}, u32[]{:S(2)}, u32[]{:S(2)}) collective-permute-start(bf16[4,32,6272]{2,1,0:T(8,128)(2,1)S(1)} %slice.65), channel_id=1, source_target_pairs={{0,2},{1,3},{2,0},{3,1},{4,6},{5,7},{6,4},{7,5},{8,10},{9,11},{10,... | collective-permute-start | bytes 4816904 | tf_op jit(solution)/shard_map/ppermute | solution.py:108
  163.5 34.8 %collective-permute-start.6 = (bf16[4,32,6272]{2,1,0:T(8,128)(2,1)S(1)}, bf16[4,32,6272]{2,1,0:T(8,128)(2,1)S(1)}, u32[]{:S(2)}, u32[]{:S(2)}) collective-permute-start(bf16[4,32,6272]{2,1,0:T(8,128)(2,1)S(1)} %slice.66), channel_id=1, source_target_pairs={{0,1},{1,0},{2,3},{3,2},{4,5},{5,4},{6,7},{7,6},{8,9},{9,8},{10,11... | collective-permute-start | bytes 4816904 | tf_op jit(solution)/shard_map/ppermute | solution.py:109
  213.0 8.5 %copy-start.3 = (bf16[16,48,2048]{2,1,0:T(8,128)(2,1)}, bf16[16,48,2048]{2,1,0:T(8,128)(2,1)S(1)}, u32[]{:S(2)}) copy-start(bf16[16,48,2048]{2,1,0:T(8,128)(2,1)S(1)} %fusion.13) | copy-start | bytes 9437188
  213.2 4.1 %copy-start.8 = (bf16[1,1,768,2048]{3,2,1,0:T(8,128)(2,1)S(1)}, bf16[1,1,768,2048]{3,2,1,0:T(8,128)(2,1)}, u32[]{:S(2)}) copy-start(bf16[1,1,768,2048]{3,2,1,0:T(8,128)(2,1)} %param.21) | copy-start | bytes 9437188
  217.3 4.1 %copy-start.9 = (bf16[1,1,2048,768]{3,2,1,0:T(8,128)(2,1)S(1)}, bf16[1,1,2048,768]{3,2,1,0:T(8,128)(2,1)}, u32[]{:S(2)}) copy-start(bf16[1,1,2048,768]{3,2,1,0:T(8,128)(2,1)} %param.19) | copy-start | bytes 9437188
  245.8 76.0 %all-to-all-start.1 = ((bf16[16,48,2048]{2,1,0:T(8,128)(2,1)}), bf16[16,48,2048]{2,1,0:T(8,128)(2,1)}, u32[]{:S(2)}, u32[]{:S(2)}) async-start(bf16[16,48,2048]{2,1,0:T(8,128)(2,1)} %bitcast.188), calls=%async_computation.1 | async-start | bytes 6291456 | tf_op jit(solution)/shard_map/all_to_all | solution.py:183
  254.4 1.7 copy-start.4
  321.8 74.5 %all-to-all-start = ((bf16[16,48,2048]{2,1,0:T(8,128)(2,1)}), bf16[16,48,2048]{2,1,0:T(8,128)(2,1)}, u32[]{:S(2)}, u32[]{:S(2)}) async-start(bf16[16,48,2048]{2,1,0:T(8,128)(2,1)} %bitcast.187), calls=%async_computation | async-start | bytes 6291456 | tf_op jit(solution)/shard_map/all_to_all | solution.py:175
  330.1 4.4 %copy-start.1 = (bf16[1,64,2048]{2,1,0:T(8,128)(2,1)S(1)}, bf16[1,64,2048]{2,1,0:T(8,128)(2,1)}, u32[]{:S(2)}) copy-start(bf16[1,64,2048]{2,1,0:T(8,128)(2,1)} %param.14) | copy-start | bytes 786436
  330.1 4.6 %copy-start.6 = (bf16[1,64,2048]{2,1,0:T(8,128)(2,1)S(1)}, bf16[1,64,2048]{2,1,0:T(8,128)(2,1)}, u32[]{:S(2)}) copy-start(bf16[1,64,2048]{2,1,0:T(8,128)(2,1)} %param.15) | copy-start | bytes 786436
  330.1 4.6 %copy-start.7 = (f32[64]{0:T(128)S(1)}, f32[64]{0:T(128)}, u32[]{:S(2)}) copy-start(f32[64]{0:T(128)} %get-tuple-element.13) | copy-start | bytes 772
  335.7 66.7 %collective-permute-start.8 = (bf16[1,64,2048]{2,1,0:T(8,128)(2,1)}, bf16[1,64,2048]{2,1,0:T(8,128)(2,1)S(1)}, u32[]{:S(2)}, u32[]{:S(2)}) collective-permute-start(bf16[1,64,2048]{2,1,0:T(8,128)(2,1)} %fusion.66), channel_id=1, source_target_pairs={{16,0},{0,16},{17,1},{1,17},{18,2},{2,18},{19,3},{3,19},{20,4},{4,... | collective-permute-start | bytes 786440 | tf_op jit(solution)/shard_map/ppermute | solution.py:12
  396.3 4.5 %copy-start.5 = (bf16[1,64,2048]{2,1,0:T(8,128)(2,1)S(1)}, bf16[1,64,2048]{2,1,0:T(8,128)(2,1)}, u32[]{:S(2)}) copy-start(bf16[1,64,2048]{2,1,0:T(8,128)(2,1)} %param.11) | copy-start | bytes 786436
  400.9 2.6 collective-permute-start.7
where the time goes:
time: 406 us; the launch traced here: 405 us
  waiting for transfers between devices  256 us (63%)
  matrix products  63.6 us (16%)
  local copies, waits for them, and re-layouts  40.1 us (10%)
  other arithmetic  24 us (6%)
  starting transfers between devices  20 us (5%)
    ppermute x3, waiting for transfers between devices, gather_ep(): got = lax.ppermute(v, axis_name, _pairs(n, n2, 1, lambda a: (a + d) % n1))  61.8 us
    ppermute x1, waiting for transfers between devices, gather_ep(): px = lax.ppermute(s1, axis_name, _pairs(n, n2, 2, flip_x))  59.1 us
    all_to_all x1, waiting for transfers between devices, local(): lax.all_to_all(made_f, 'ep', split_axis=0, concat_axis=0, tiled=True)  58.8 us
    all_to_all x1, waiting for transfers between devices, local(): lax.all_to_all(made_b, 'ep', split_axis=0, concat_axis=0, tiled=True)  49.7 us
    ppermute x1, waiting for transfers between devices, gather_ep(): d1 = lax.ppermute(px[:, :h], axis_name, _pairs(n, n2, 2, flip_y))  24.3 us
    dot_general x1, matrix products, expert_backward(): jnp.dot(dgate, w_g.T, preferred_element_type=jnp.float32)  12.9 us
    dot_general x1, matrix products, expert_forward(): jnp.dot(act, w_d, preferred_element_type=jnp.float32).astype(jnp.bfloat16)  11.9 us
    dot_general x3, matrix products, pick_rows(): jnp.einsum('bct,btd->bcd', onehot, rows, preferred_element_type=jnp.float32)  10.4 us
  transfers between devices with their start and end apart: 11, of which 9 were waited for; matrix products, arithmetic and copies ran while one was open for 15% of the time, Pallas kernels for 0%

commit v1 on v0

--- a/solution.py
+++ b/solution.py
@@ -4,6 +4,28 @@
 from jax.sharding import PartitionSpec as P
 
 EPS = 1e-06
+
+
+def in_blocks(x, dim, size):
+    before, after = (x.shape[:dim], x.shape[dim + 1 :])
+    return jnp.moveaxis(x.reshape(*before, size, -1, *after), dim, 0)
+
+
+def joined_along(blocks, dim):
+    dims = list(blocks.shape[1:])
+    dims[dim] *= blocks.shape[0]
+    return jnp.moveaxis(blocks, 0, dim).reshape(dims)
+
+
+def pairwise_exchange(x, axis, split_dim, concat_dim):
+    peers, here = (lax.axis_size(axis), lax.axis_index(axis))
+    blocks = in_blocks(x, split_dim, peers)
+    gathered = [blocks[here]]
+    for step in range(1, peers):
+        sent = blocks[here ^ step]
+        gathered.append(lax.ppermute(sent, axis, [(i, i ^ step) for i in range(peers)]))
+    blocks = jnp.stack(gathered)[here ^ jnp.arange(peers)]
+    return joined_along(blocks, concat_dim)
 
 
 def from_behind(block, axis, distance):
@@ -180,7 +202,7 @@
         (slot_w_b[:, :, None] * g_rows.astype(jnp.float32)).astype(jnp.bfloat16).reshape(-1, width)
     )
     made_b = expert_backward(rows, cots, w_g, w_u, w_d).reshape(n_exp, cap, width)
-    back_b = lax.all_to_all(made_b, "ep", split_axis=0, concat_axis=0, tiled=True)
+    back_b = pairwise_exchange(made_b, "ep", 0, 0)
     places_f = slot_places(ids_fwd[0], n_exp, cap)
     picked_f = combine_rows(places_f, back_f.reshape(-1, width), top)
     mixed = jnp.sum(weights_f[:, :, None] * picked_f, axis=1)

time: 406 us -> 440 us (1.084)
  starting transfers between devices: 20 us -> 46.4 us
  local copies, waits for them, and re-layouts: 40.1 us -> 61.7 us
  waiting for transfers between devices: 256 us -> 239 us
    ppermute x0 -> x15, waiting for transfers between devices: none -> 96.7 us  [pairwise_exchange(): lax.ppermute(sent, axis, [(i, i ^ step) for i in range(peers)])]
    all_to_all x1, waiting for transfers between devices: 58.8 us -> 0.01 us  [local(): lax.all_to_all(made_f, 'ep', split_axis=0, concat_axis=0, tiled=True)]
    all_to_all x1 -> x0, waiting for transfers between devices: 49.7 us -> none  [local(): lax.all_to_all(made_b, 'ep', split_axis=0, concat_axis=0, tiled=True)]
    ppermute x0 -> x15, starting transfers between devices: none -> 32.9 us  [pairwise_exchange(): lax.ppermute(sent, axis, [(i, i ^ step) for i in range(peers)])]
    unnamed x24 -> x48, local copies, waits for them, and re-layouts: 4.66 us -> 19 us
    ppermute x1, waiting for transfers between devices: 59.1 us -> 53.5 us  [gather_ep(): px = lax.ppermute(s1, axis_name, _pairs(n, n2, 2, flip_x))]
    all_to_all x1 -> x0, starting transfers between devices: 5.3 us -> none  [local(): lax.all_to_all(made_b, 'ep', split_axis=0, concat_axis=0, tiled=True)]
  transfers between devices with their start and end apart: 11 -> 25, of which waited for: 9 -> 15; matrix products, arithmetic and copies ran while one was open for 15% -> 19% of each run, Pallas kernels for 0% -> 0%
where the time goes in v1:
time: 440 us; the launch traced here: 439 us
  waiting for transfers between devices  239 us (54%)
  matrix products  62.5 us (14%)
  local copies, waits for them, and re-layouts  61.7 us (14%)
  starting transfers between devices  46.4 us (11%)
  other arithmetic  28 us (6%)
    ppermute x15, waiting for transfers between devices, pairwise_exchange(): lax.ppermute(sent, axis, [(i, i ^ step) for i in range(peers)])  96.7 us
    ppermute x3, waiting for transfers between devices, gather_ep(): got = lax.ppermute(v, axis_name, _pairs(n, n2, 1, lambda a: (a + d) % n1))  61.7 us
    ppermute x1, waiting for transfers between devices, gather_ep(): px = lax.ppermute(s1, axis_name, _pairs(n, n2, 2, flip_x))  53.5 us
    ppermute x15, starting transfers between devices, pairwise_exchange(): lax.ppermute(sent, axis, [(i, i ^ step) for i in range(peers)])  32.9 us
    ppermute x1, waiting for transfers between devices, gather_ep(): d1 = lax.ppermute(px[:, :h], axis_name, _pairs(n, n2, 2, flip_y))  24.3 us
    unnamed x48, local copies, waits for them, and re-layouts  19 us
    dot_general x1, matrix products, expert_backward(): jnp.dot(dgate, w_g.T, preferred_element_type=jnp.float32)  12.9 us
    dot_general x1, matrix products, expert_forward(): jnp.dot(act, w_d, preferred_element_type=jnp.float32).astype(jnp.bfloat16)  11.9 us
  transfers between devices with their start and end apart: 25, of which 15 were waited for; matrix products, arithmetic and copies ran while one was open for 19% of the time, Pallas kernels for 0%

profile of v1, /device:TPU:13, one launch (start us, length us, event | category | flops | bytes accessed | tf_op | source)
XLA Modules:
  0.0 438.6 jit_solution(1428492697700257810)
XLA Ops:
  10.4 1.9 fusion.61
  12.8 2.0 concatenate.11
  18.7 1.9 broadcast_in_dim.78
  21.7 12.3 %collective-permute-done = bf16[64,6272]{1,0:T(8,128)(2,1)} collective-permute-done((bf16[64,6272]{1,0:T(8,128)(2,1)}, bf16[64,6272]{1,0:T(8,128)(2,1)}, u32[]{:S(2)}, u32[]{:S(2)}) %collective-permute-start) | collective-permute-done | bytes 802848 | tf_op jit(solution)/shard_map/ppermute | solution.py:123
  34.0 2.1 bitcast_dynamic-update-slice_fusion.5
  36.1 48.6 %collective-permute-done.1 = bf16[64,6272]{1,0:T(8,128)(2,1)} collective-permute-done((bf16[64,6272]{1,0:T(8,128)(2,1)}, bf16[64,6272]{1,0:T(8,128)(2,1)}, u32[]{:S(2)}, u32[]{:S(2)}) %collective-permute-start.1) | collective-permute-done | bytes 802848 | tf_op jit(solution)/shard_map/ppermute | solution.py:123
  84.7 2.1 bitcast_dynamic-update-slice_fusion.4
  87.5 2.1 bitcast_dynamic-update-slice_fusion.3
  96.6 6.2 %broadcast_in_dim.77 = bf16[4,4,64,6272]{3,2,0,1:T(8,128)(2,1)} broadcast(bf16[]{:T(256)} %constant.103.clone.1), dimensions={} | broadcast | bytes 12845058 | tf_op jit(solution)/shard_map/broadcast_in_dim | solution.py:133
  102.8 3.8 bitcast_dynamic-update-slice_fusion.2
  106.7 53.5 %collective-permute-done.3 = bf16[4,64,6272]{2,1,0:T(8,128)(2,1)} collective-permute-done((bf16[4,64,6272]{2,1,0:T(8,128)(2,1)}, bf16[4,64,6272]{2,1,0:T(8,128)(2,1)}, u32[]{:S(2)}, u32[]{:S(2)}) %collective-permute-start.3) | collective-permute-done | bytes 3211296 | tf_op jit(solution)/shard_map/ppermute | solution.py:127
  164.8 3.8 bitcast_dynamic-update-slice_fusion.1
  168.6 3.8 bitcast_dynamic-update-slice_fusion
  172.5 24.3 %collective-permute-done.5 = bf16[4,32,6272]{2,1,0:T(8,128)(2,1)S(1)} collective-permute-done((bf16[4,32,6272]{2,1,0:T(8,128)(2,1)S(1)}, bf16[4,32,6272]{2,1,0:T(8,128)(2,1)S(1)}, u32[]{:S(2)}, u32[]{:S(2)}) %collective-permute-start.5) | collective-permute-done | bytes 1605664 | tf_op jit(solution)/shard_map/ppermute | solution.py:130
  198.3 1.9 fusion.16
  201.3 1.9 fusion.88
  203.2 6.4 %fusion.96 = f32[16,64]{1,0:T(8,128)S(1)} fusion(f32[16,64,24]{2,1,0:T(8,128)S(1)} %slice_convert_fusion, s32[]{:T(128)S(6)} %axis_index.8, bf16[16,64,6272]{2,1,0:T(8,128)(2,1)} %bitcast.242), kind=kOutput, calls=%fused_computation.170 | output fusion | flops 57351 | bytes 1593348 | tf_op jit(solution)/shard_map/div | solution.py:193
  209.9 3.1 fusion.13
  213.2 4.1 multiply_convert_fusion
  217.4 4.1 fusion.17
  221.5 4.0 fusion.27
  225.5 12.9 %fusion.25 = f32[768,2048]{1,0:T(8,128)} fusion(bf16[1,1,2048,768]{3,2,1,0:T(8,128)(2,1)} %param.19, f32[768,768]{1,0:T(8,128)} %fusion.27, f32[768,768]{1,0:T(8,128)} %fusion.17, bf16[768,2048]{1,0:T(8,128)(2,1)} %bitcast.248, bf16[1,1,2048,768]{3,2,1,0:T(8,128)(2,1)S(1)} %copy-done), kind=kOutput, calls=%fused_computation.28 | convolution fusion | flops 4837736448 | bytes 20447232 | tf_op jit(solution)/shard_map/dot_general | solution.py:65
  238.5 6.2 %add_convert_fusion = bf16[768,2048]{1,0:T(8,128)(2,1)S(1)} fusion(f32[768,2048]{1,0:T(8,128)} %fusion.25, bf16[1,1,2048,768]{3,2,1,0:T(8,128)(2,1)S(1)} %copy-done, f32[768,768]{1,0:T(8,128)} %fusion.17, f32[768,768]{1,0:T(8,128)} %fusion.27), kind=kOutput, calls=%fused_computation.2 | convolution fusion | flops 2422603776 | bytes 17301504 | tf_op jit(solution)/shard_map/dot_general | solution.py:65
  249.0 2.4 collective-permute-start.12
  254.2 3.1 fusion.7
  257.3 1.7 copy-done.4
  259.0 4.0 fusion.23
  263.0 11.9 %convolution_convert_fusion = bf16[768,2048]{1,0:T(8,128)(2,1)} fusion(bf16[1,1,768,2048]{3,2,1,0:T(8,128)(2,1)} %param.21, f32[768,768]{1,0:T(8,128)} %fusion.23, bf16[768,2048]{1,0:T(8,128)(2,1)} %bitcast.250, bf16[1,1,2048,768]{3,2,1,0:T(8,128)(2,1)} %param.19), kind=kOutput, calls=%fused_computation.14 | convolution fusion | flops 4836950016 | bytes 14942208 | tf_op jit(solution)/shard_map/dot_general | solution.py:55
  274.9 5.2 %all-to-all-start = ((bf16[16,48,2048]{2,1,0:T(8,128)(2,1)}), bf16[16,48,2048]{2,1,0:T(8,128)(2,1)}, u32[]{:S(2)}, u32[]{:S(2)}) async-start(bf16[16,48,2048]{2,1,0:T(8,128)(2,1)} %bitcast.251), calls=%async_computation | async-start | bytes 6291456 | tf_op jit(solution)/shard_map/all_to_all | solution.py:197
  280.7 1.6 bitcast_dynamic-update-slice_fusion.21
  282.3 2.8 collective-permute-start.14
  285.1 1.6 bitcast_dynamic-update-slice_fusion.20
  286.7 2.1 collective-permute-start.15
  292.3 2.1 collective-permute-start.17
  296.0 38.6 %collective-permute-done.13 = bf16[1,48,2048]{2,1,0:T(8,128)(2,1)S(1)} collective-permute-done((bf16[1,48,2048]{2,1,0:T(8,128)(2,1)}, bf16[1,48,2048]{2,1,0:T(8,128)(2,1)S(1)}, u32[]{:S(2)}, u32[]{:S(2)}) %collective-permute-start.13) | collective-permute-done | bytes 196640 | tf_op jit(solution)/shard_map/ppermute | solution.py:26
  335.3 3.0 collective-permute-done.14
  338.3 2.3 collective-permute-start.19
  341.3 29.3 %collective-permute-done.15 = bf16[1,48,2048]{2,1,0:T(8,128)(2,1)S(1)} collective-permute-done((bf16[1,48,2048]{2,1,0:T(8,128)(2,1)}, bf16[1,48,2048]{2,1,0:T(8,128)(2,1)S(1)}, u32[]{:S(2)}, u32[]{:S(2)}) %collective-permute-start.15) | collective-permute-done | bytes 196640 | tf_op jit(solution)/shard_map/ppermute | solution.py:26
  370.6 4.3 collective-permute-start.20
  375.7 3.9 collective-permute-start.21
  381.2 9.5 %collective-permute-start.22 = (bf16[1,48,2048]{2,1,0:T(8,128)(2,1)S(1)}, bf16[1,48,2048]{2,1,0:T(8,128)(2,1)S(1)}, u32[]{:S(2)}, u32[]{:S(2)}) collective-permute-start(bf16[1,48,2048]{2,1,0:T(8,128)(2,1)S(1)} %get-tuple-element.4), channel_id=1, source_target_pairs={{0,15},{1,14},{2,13},{3,12},{4,11},{5,10},{6,9},{7,8},{8,7},{9,6},... | collective-permute-start | bytes 589832 | tf_op jit(solution)/shard_map/ppermute | solution.py:26
  392.1 13.2 %collective-permute-done.19 = bf16[1,48,2048]{2,1,0:T(8,128)(2,1)S(1)} collective-permute-done((bf16[1,48,2048]{2,1,0:T(8,128)(2,1)}, bf16[1,48,2048]{2,1,0:T(8,128)(2,1)S(1)}, u32[]{:S(2)}, u32[]{:S(2)}) %collective-permute-start.19) | collective-permute-done | bytes 196640 | tf_op jit(solution)/shard_map/ppermute | solution.py:26
  406.0 4.4 collective-permute-done.20
  411.1 3.2 collective-permute-done.21
  415.0 3.9 collective-permute-done.22
  419.6 4.3 gather_fusion
  424.0 4.3 convolution_reduce_fusion
  431.0 4.5 %multiply_reduce_fusion = f32[64,2048]{1,0:T(8,128)S(1)} fusion(bf16[768,2048,1]{1,0,2:T(8,128)(2,1)} %bitcast.31, f32[64,8]{1,0:T(8,128)S(1)} %copy-done.9, s32[64,8]{1,0:T(8,128)S(1)} %copy-done.7), kind=kOutput, calls=%fused_computation.10 | convolution fusion | flops 1612972032 | bytes 3674112 | tf_op jit(solution)/shard_map/dot_general | solution.py:96
  (130 shorter events, 56.7 us)
Async XLA Ops:
  0.6 224.9 %copy-start = (bf16[1,1,2048,768]{3,2,1,0:T(8,128)(2,1)S(1)}, bf16[1,1,2048,768]{3,2,1,0:T(8,128)(2,1)}, u32[]{:S(2)}) copy-start(bf16[1,1,2048,768]{3,2,1,0:T(8,128)(2,1)} %param.20) | copy-start | bytes 9437188
  9.7 0.6 copy-start.10
  14.9 19.1 %collective-permute-start = (bf16[64,6272]{1,0:T(8,128)(2,1)}, bf16[64,6272]{1,0:T(8,128)(2,1)}, u32[]{:S(2)}, u32[]{:S(2)}) collective-permute-start(bf16[64,6272]{1,0:T(8,128)(2,1)} %concatenate.11), channel_id=1, source_target_pairs={{0,4},{1,5},{2,6},{3,7},{4,8},{5,9},{6,10},{7,11},{8,12},{9,13},{1... | collective-permute-start | bytes 2408456 | tf_op jit(solution)/shard_map/ppermute | solution.py:123
  16.2 68.5 %collective-permute-start.1 = (bf16[64,6272]{1,0:T(8,128)(2,1)}, bf16[64,6272]{1,0:T(8,128)(2,1)}, u32[]{:S(2)}, u32[]{:S(2)}) collective-permute-start(bf16[64,6272]{1,0:T(8,128)(2,1)} %concatenate.11), channel_id=1, source_target_pairs={{0,8},{1,9},{2,10},{3,11},{4,12},{5,13},{6,14},{7,15},{8,0},{9,1},... | collective-permute-start | bytes 2408456 | tf_op jit(solution)/shard_map/ppermute | solution.py:123
  17.3 70.3 %collective-permute-start.2 = (bf16[64,6272]{1,0:T(8,128)(2,1)}, bf16[64,6272]{1,0:T(8,128)(2,1)}, u32[]{:S(2)}, u32[]{:S(2)}) collective-permute-start(bf16[64,6272]{1,0:T(8,128)(2,1)} %concatenate.11), channel_id=1, source_target_pairs={{0,12},{1,13},{2,14},{3,15},{4,0},{5,1},{6,2},{7,3},{8,4},{9,5},{1... | collective-permute-start | bytes 2408456 | tf_op jit(solution)/shard_map/ppermute | solution.py:123
  18.7 2.0 copy-start.2
  89.6 70.6 %collective-permute-start.3 = (bf16[4,64,6272]{2,1,0:T(8,128)(2,1)}, bf16[4,64,6272]{2,1,0:T(8,128)(2,1)}, u32[]{:S(2)}, u32[]{:S(2)}) collective-permute-start(bf16[4,64,6272]{2,1,0:T(8,128)(2,1)} %bitcast_dynamic-update-slice_fusion.3), channel_id=1, source_target_pairs={{0,1},{1,0},{2,3},{3,2},{4,5},{5,4},{6,7},{7,6},{8,9},{9,8},{10,11... | collective-permute-start | bytes 9633800 | tf_op jit(solution)/shard_map/ppermute | solution.py:127
  90.8 71.2 %collective-permute-start.4 = (bf16[4,64,6272]{2,1,0:T(8,128)(2,1)}, bf16[4,64,6272]{2,1,0:T(8,128)(2,1)}, u32[]{:S(2)}, u32[]{:S(2)}) collective-permute-start(bf16[4,64,6272]{2,1,0:T(8,128)(2,1)} %bitcast_dynamic-update-slice_fusion.3), channel_id=1, source_target_pairs={{0,2},{1,3},{2,0},{3,1},{4,6},{5,7},{6,4},{7,5},{8,10},{9,11},{10,... | collective-permute-start | bytes 9633800 | tf_op jit(solution)/shard_map/ppermute | solution.py:128
  161.7 35.0 %collective-permute-start.5 = (bf16[4,32,6272]{2,1,0:T(8,128)(2,1)S(1)}, bf16[4,32,6272]{2,1,0:T(8,128)(2,1)S(1)}, u32[]{:S(2)}, u32[]{:S(2)}) collective-permute-start(bf16[4,32,6272]{2,1,0:T(8,128)(2,1)S(1)} %slice.67), channel_id=1, source_target_pairs={{0,2},{1,3},{2,0},{3,1},{4,6},{5,7},{6,4},{7,5},{8,10},{9,11},{10,... | collective-permute-start | bytes 4816904 | tf_op jit(solution)/shard_map/ppermute | solution.py:130
  163.5 34.8 %collective-permute-start.6 = (bf16[4,32,6272]{2,1,0:T(8,128)(2,1)S(1)}, bf16[4,32,6272]{2,1,0:T(8,128)(2,1)S(1)}, u32[]{:S(2)}, u32[]{:S(2)}) collective-permute-start(bf16[4,32,6272]{2,1,0:T(8,128)(2,1)S(1)} %slice.68), channel_id=1, source_target_pairs={{0,1},{1,0},{2,3},{3,2},{4,5},{5,4},{6,7},{7,6},{8,9},{9,8},{10,11... | collective-permute-start | bytes 4816904 | tf_op jit(solution)/shard_map/ppermute | solution.py:131
  213.0 8.5 %copy-start.3 = (bf16[16,48,2048]{2,1,0:T(8,128)(2,1)}, bf16[16,48,2048]{2,1,0:T(8,128)(2,1)S(1)}, u32[]{:S(2)}) copy-start(bf16[16,48,2048]{2,1,0:T(8,128)(2,1)S(1)} %fusion.13) | copy-start | bytes 9437188
  213.2 4.2 copy-start.13
  217.4 4.1 copy-start.14
  246.3 33.8 %collective-permute-start.8 = (bf16[1,48,2048]{2,1,0:T(8,128)(2,1)}, bf16[1,48,2048]{2,1,0:T(8,128)(2,1)}, u32[]{:S(2)}, u32[]{:S(2)}) collective-permute-start(bf16[1,48,2048]{2,1,0:T(8,128)(2,1)} %get-tuple-element.18), channel_id=1, source_target_pairs={{0,1},{1,0},{2,3},{3,2},{4,5},{5,4},{6,7},{7,6},{8,9},{9,8},{10,11... | collective-permute-start | bytes 589832 | tf_op jit(solution)/shard_map/ppermute | solution.py:26
  247.5 34.8 %collective-permute-start.9 = (bf16[1,48,2048]{2,1,0:T(8,128)(2,1)}, bf16[1,48,2048]{2,1,0:T(8,128)(2,1)}, u32[]{:S(2)}, u32[]{:S(2)}) collective-permute-start(bf16[1,48,2048]{2,1,0:T(8,128)(2,1)} %get-tuple-element.17), channel_id=1, source_target_pairs={{0,2},{1,3},{2,0},{3,1},{4,6},{5,7},{6,4},{7,5},{8,10},{9,11},{10,... | collective-permute-start | bytes 589832 | tf_op jit(solution)/shard_map/ppermute | solution.py:26
  248.8 38.0 %collective-permute-start.10 = (bf16[1,48,2048]{2,1,0:T(8,128)(2,1)}, bf16[1,48,2048]{2,1,0:T(8,128)(2,1)}, u32[]{:S(2)}, u32[]{:S(2)}) collective-permute-start(bf16[1,48,2048]{2,1,0:T(8,128)(2,1)} %get-tuple-element.16), channel_id=1, source_target_pairs={{0,3},{1,2},{2,1},{3,0},{4,7},{5,6},{6,5},{7,4},{8,11},{9,10},{10,... | collective-permute-start | bytes 589832 | tf_op jit(solution)/shard_map/ppermute | solution.py:26
  248.9 41.5 %collective-permute-start.11 = (bf16[1,48,2048]{2,1,0:T(8,128)(2,1)}, bf16[1,48,2048]{2,1,0:T(8,128)(2,1)}, u32[]{:S(2)}, u32[]{:S(2)}) collective-permute-start(bf16[1,48,2048]{2,1,0:T(8,128)(2,1)} %get-tuple-element.15), channel_id=1, source_target_pairs={{0,4},{1,5},{2,6},{3,7},{4,0},{5,1},{6,2},{7,3},{8,12},{9,13},{10,... | collective-permute-start | bytes 589832 | tf_op jit(solution)/shard_map/ppermute | solution.py:26
  249.0 43.4 %collective-permute-start.12 = (bf16[1,48,2048]{2,1,0:T(8,128)(2,1)}, bf16[1,48,2048]{2,1,0:T(8,128)(2,1)}, u32[]{:S(2)}, u32[]{:S(2)}) collective-permute-start(bf16[1,48,2048]{2,1,0:T(8,128)(2,1)} %get-tuple-element.14), channel_id=1, source_target_pairs={{0,5},{1,4},{2,7},{3,6},{4,1},{5,0},{6,3},{7,2},{8,13},{9,12},{10,... | collective-permute-start | bytes 589832 | tf_op jit(solution)/shard_map/ppermute | solution.py:26
  257.3 1.7 copy-start.4
  274.9 156.1 %all-to-all-start = ((bf16[16,48,2048]{2,1,0:T(8,128)(2,1)}), bf16[16,48,2048]{2,1,0:T(8,128)(2,1)}, u32[]{:S(2)}, u32[]{:S(2)}) async-start(bf16[16,48,2048]{2,1,0:T(8,128)(2,1)} %bitcast.251), calls=%async_computation | async-start | bytes 6291456 | tf_op jit(solution)/shard_map/all_to_all | solution.py:197
  280.1 54.5 %collective-permute-start.13 = (bf16[1,48,2048]{2,1,0:T(8,128)(2,1)}, bf16[1,48,2048]{2,1,0:T(8,128)(2,1)S(1)}, u32[]{:S(2)}, u32[]{:S(2)}) collective-permute-start(bf16[1,48,2048]{2,1,0:T(8,128)(2,1)} %get-tuple-element.13), channel_id=1, source_target_pairs={{0,6},{1,7},{2,4},{3,5},{4,2},{5,3},{6,0},{7,1},{8,14},{9,15},{10,... | collective-permute-start | bytes 589832 | tf_op jit(solution)/shard_map/ppermute | solution.py:26
  282.3 56.0 %collective-permute-start.14 = (bf16[1,48,2048]{2,1,0:T(8,128)(2,1)}, bf16[1,48,2048]{2,1,0:T(8,128)(2,1)S(1)}, u32[]{:S(2)}, u32[]{:S(2)}) collective-permute-start(bf16[1,48,2048]{2,1,0:T(8,128)(2,1)} %get-tuple-element.12), channel_id=1, source_target_pairs={{0,7},{1,6},{2,5},{3,4},{4,3},{5,2},{6,1},{7,0},{8,15},{9,14},{10,... | collective-permute-start | bytes 589832 | tf_op jit(solution)/shard_map/ppermute | solution.py:26
  286.7 83.9 %collective-permute-start.15 = (bf16[1,48,2048]{2,1,0:T(8,128)(2,1)}, bf16[1,48,2048]{2,1,0:T(8,128)(2,1)S(1)}, u32[]{:S(2)}, u32[]{:S(2)}) collective-permute-start(bf16[1,48,2048]{2,1,0:T(8,128)(2,1)} %get-tuple-element.11), channel_id=1, source_target_pairs={{0,8},{1,9},{2,10},{3,11},{4,12},{5,13},{6,14},{7,15},{8,0},{9,1},... | collective-permute-start | bytes 589832 | tf_op jit(solution)/shard_map/ppermute | solution.py:26
  290.5 85.2 %collective-permute-start.16 = (bf16[1,48,2048]{2,1,0:T(8,128)(2,1)}, bf16[1,48,2048]{2,1,0:T(8,128)(2,1)S(1)}, u32[]{:S(2)}, u32[]{:S(2)}) collective-permute-start(bf16[1,48,2048]{2,1,0:T(8,128)(2,1)} %get-tuple-element.10), channel_id=1, source_target_pairs={{0,9},{1,8},{2,11},{3,10},{4,13},{5,12},{6,15},{7,14},{8,1},{9,0},... | collective-permute-start | bytes 589832 | tf_op jit(solution)/shard_map/ppermute | solution.py:26
  292.3 88.9 %collective-permute-start.17 = (bf16[1,48,2048]{2,1,0:T(8,128)(2,1)}, bf16[1,48,2048]{2,1,0:T(8,128)(2,1)S(1)}, u32[]{:S(2)}, u32[]{:S(2)}) collective-permute-start(bf16[1,48,2048]{2,1,0:T(8,128)(2,1)} %get-tuple-element.9), channel_id=1, source_target_pairs={{0,10},{1,11},{2,8},{3,9},{4,14},{5,15},{6,12},{7,13},{8,2},{9,3},... | collective-permute-start | bytes 589832 | tf_op jit(solution)/shard_map/ppermute | solution.py:26
  334.6 56.7 %collective-permute-start.18 = (bf16[1,48,2048]{2,1,0:T(8,128)(2,1)}, bf16[1,48,2048]{2,1,0:T(8,128)(2,1)S(1)}, u32[]{:S(2)}, u32[]{:S(2)}) collective-permute-start(bf16[1,48,2048]{2,1,0:T(8,128)(2,1)} %get-tuple-element.8), channel_id=1, source_target_pairs={{0,11},{1,10},{2,9},{3,8},{4,15},{5,14},{6,13},{7,12},{8,3},{9,2},... | collective-permute-start | bytes 589832 | tf_op jit(solution)/shard_map/ppermute | solution.py:26
  338.3 67.0 %collective-permute-start.19 = (bf16[1,48,2048]{2,1,0:T(8,128)(2,1)}, bf16[1,48,2048]{2,1,0:T(8,128)(2,1)S(1)}, u32[]{:S(2)}, u32[]{:S(2)}) collective-permute-start(bf16[1,48,2048]{2,1,0:T(8,128)(2,1)} %get-tuple-element.7), channel_id=1, source_target_pairs={{0,12},{1,13},{2,14},{3,15},{4,8},{5,9},{6,10},{7,11},{8,4},{9,5},... | collective-permute-start | bytes 589832 | tf_op jit(solution)/shard_map/ppermute | solution.py:26
  370.6 39.7 %collective-permute-start.20 = (bf16[1,48,2048]{2,1,0:T(8,128)(2,1)}, bf16[1,48,2048]{2,1,0:T(8,128)(2,1)S(1)}, u32[]{:S(2)}, u32[]{:S(2)}) collective-permute-start(bf16[1,48,2048]{2,1,0:T(8,128)(2,1)} %get-tuple-element.6), channel_id=1, source_target_pairs={{0,13},{1,12},{2,15},{3,14},{4,9},{5,8},{6,11},{7,10},{8,5},{9,4},... | collective-permute-start | bytes 589832 | tf_op jit(solution)/shard_map/ppermute | solution.py:26
  375.7 38.6 %collective-permute-start.21 = (bf16[1,48,2048]{2,1,0:T(8,128)(2,1)S(1)}, bf16[1,48,2048]{2,1,0:T(8,128)(2,1)S(1)}, u32[]{:S(2)}, u32[]{:S(2)}) collective-permute-start(bf16[1,48,2048]{2,1,0:T(8,128)(2,1)S(1)} %get-tuple-element.5), channel_id=1, source_target_pairs={{0,14},{1,15},{2,12},{3,13},{4,10},{5,11},{6,8},{7,9},{8,6},{9,7},... | collective-permute-start | bytes 589832 | tf_op jit(solution)/shard_map/ppermute | solution.py:26
  381.2 37.8 %collective-permute-start.22 = (bf16[1,48,2048]{2,1,0:T(8,128)(2,1)S(1)}, bf16[1,48,2048]{2,1,0:T(8,128)(2,1)S(1)}, u32[]{:S(2)}, u32[]{:S(2)}) collective-permute-start(bf16[1,48,2048]{2,1,0:T(8,128)(2,1)S(1)} %get-tuple-element.4), channel_id=1, source_target_pairs={{0,15},{1,14},{2,13},{3,12},{4,11},{5,10},{6,9},{7,8},{8,7},{9,6},... | collective-permute-start | bytes 589832 | tf_op jit(solution)/shard_map/ppermute | solution.py:26
  419.6 4.3 copy-start.8
  424.0 4.4 %copy-start.1 = (bf16[1,64,2048]{2,1,0:T(8,128)(2,1)S(1)}, bf16[1,64,2048]{2,1,0:T(8,128)(2,1)}, u32[]{:S(2)}) copy-start(bf16[1,64,2048]{2,1,0:T(8,128)(2,1)} %param.14) | copy-start | bytes 786436
  424.0 4.6 %copy-start.6 = (bf16[1,64,2048]{2,1,0:T(8,128)(2,1)S(1)}, bf16[1,64,2048]{2,1,0:T(8,128)(2,1)}, u32[]{:S(2)}) copy-start(bf16[1,64,2048]{2,1,0:T(8,128)(2,1)} %param.15) | copy-start | bytes 786436
  424.0 4.6 %copy-start.11 = (f32[64]{0:T(128)S(1)}, f32[64]{0:T(128)}, u32[]{:S(2)}) copy-start(f32[64]{0:T(128)} %copy-done.10) | copy-start | bytes 772
  424.0 4.6 %copy-start.12 = (f32[64]{0:T(128)S(1)}, f32[64]{0:T(128)}, u32[]{:S(2)}) copy-start(f32[64]{0:T(128)} %get-tuple-element.29) | copy-start | bytes 772
  424.0 7.0 %copy-start.7 = (s32[64,8]{1,0:T(8,128)S(1)}, s32[64,8]{1,0:T(8,128)}, u32[]{:S(2)}) copy-start(s32[64,8]{1,0:T(8,128)} %bitcast_add_fusion.1) | copy-start | bytes 6148
  424.0 7.0 %copy-start.9 = (f32[64,8]{1,0:T(8,128)S(1)}, f32[64,8]{1,0:T(8,128)}, u32[]{:S(2)}) copy-start(f32[64,8]{1,0:T(8,128)} %copy.37) | copy-start | bytes 6148
  429.6 6.1 %collective-permute-start.23 = (bf16[1,64,2048]{2,1,0:T(8,128)(2,1)}, bf16[1,64,2048]{2,1,0:T(8,128)(2,1)S(1)}, u32[]{:S(2)}, u32[]{:S(2)}) collective-permute-start(bf16[1,64,2048]{2,1,0:T(8,128)(2,1)} %fusion.66), channel_id=1, source_target_pairs={{16,0},{0,16},{17,1},{1,17},{18,2},{2,18},{19,3},{3,19},{20,4},{4,... | collective-permute-start | bytes 786440 | tf_op jit(solution)/shard_map/ppermute | solution.py:34
  431.0 4.5 %copy-start.5 = (bf16[1,64,2048]{2,1,0:T(8,128)(2,1)S(1)}, bf16[1,64,2048]{2,1,0:T(8,128)(2,1)}, u32[]{:S(2)}) copy-start(bf16[1,64,2048]{2,1,0:T(8,128)(2,1)} %param.11) | copy-start | bytes 786436
  435.5 1.6 collective-permute-start.7
